TPU v7x, 512 devices: a whole 4x8x8 slice. The times are simulated.
512 devices in a mesh: pipe: 32 (over y, z_lo), seq: 16 (over z_hi, x, core).
Axes of the slice: x: 4, y: 8, z: 8 (z_hi: 2, z_lo: 4; z = z_hi * 4 + z_lo), core: 2. Of those that a mesh axis runs over, the one named last changes fastest.
Arguments:
- x_first: bfloat16 [4096, 2560], P(('pipe', 'seq')), may hold values from -6 to 6
- x_second: bfloat16 [4096, 2560], P(('pipe', 'seq')), may hold values from -6 to 6
- stale_kv: bfloat16 [2, 4096, 2048], P(None, 'pipe', 'seq'), may hold values from -6 to 6
- w_qkv: bfloat16 [3, 2560, 2048], P(None, None, 'seq'), may hold values from -0.125 to 0.125
- w_out: bfloat16 [2048, 2560], P('seq'), may hold values from -0.125 to 0.125
- q_gain: float32 [2048], P('seq'), may hold values from 0.4 to 5
- k_gain: float32 [2048], P('seq'), may hold values from 0.4 to 5
- layout: int32 [32, 16], replicated, may hold values from 0 to 31, as said below
- counts: int32 [32], replicated, may hold values from 1 to 16, as said below
- slot_block: int32 [32], replicated, may hold values from 0 to 31, each once
Outputs:
- out_first: bfloat16 [4096, 2560], P(('pipe', 'seq'))
- out_second: bfloat16 [4096, 2560], P(('pipe', 'seq'))
Inputs may be any that keep to these rules, and one draw needn't show every extreme that they name: `layout`: entries of a row are distinct sequence blocks and the first entry of row b is b itself. `counts`: some block reads 16 entries. `slot_block`: each block once.
All inputs are finite; a program needn't handle non-finite values.
Results may differ from a plain program's by a relative error of at most 0.019.
Values may be sent and summed in bfloat16 or wider, within the bound.
No kernel may reach another device: no remote copies, remote signals or barrier semaphores. Data moves between devices by JAX's collectives and lax.ppermute only.
A program may use at most 64 MiB of HBM per device.

v0:
```python
import math
import jax
import jax.numpy as jnp
from jax import lax
from jax.sharding import PartitionSpec as P

HS = 64
BLOCK = 128
BPM = 1
HIGH = lax.Precision.HIGHEST
NEG = -1e30


def slot_mask(layout, counts, slot_block):
    total = layout.shape[0]
    width = layout.shape[1]
    blocks = jnp.arange(total, dtype=jnp.int32)
    valid = jnp.arange(width, dtype=jnp.int32)[None, :] < counts[:, None]
    member = jnp.sum(
        ((layout[:, :, None] == blocks[None, None, :]) & valid[:, :, None]).astype(jnp.float32),
        axis=1,
    )
    placed = (slot_block[:, None] == blocks[None, :]).astype(jnp.float32)
    linked = jnp.dot(jnp.dot(placed, member, precision=HIGH), placed.T, precision=HIGH)
    return linked > 0.5


def normalize(raw, gain, size):
    count = raw.shape[0]
    grid = raw.reshape(count, -1, size)
    factor = lax.rsqrt(jnp.mean(grid * grid, axis=2, keepdims=True) + 1e-06)
    return (grid * factor).reshape(count, -1) * gain[None, :]


def partial_attend(query, keys, values, allowed, scale):
    heads = query.shape[1]
    qrows = query.shape[0]
    krows = keys.shape[0]
    scores = jnp.einsum("qhd,khd->hqk", query, keys, preferred_element_type=jnp.float32) * scale
    grid = scores.reshape(heads, qrows // BLOCK, BLOCK, krows // BLOCK, BLOCK)
    keep = allowed[None, :, None, :, None]
    grid = jnp.where(keep, grid, NEG)
    top = jnp.max(grid, axis=(3, 4))
    weights = jnp.where(keep, jnp.exp(grid - top[:, :, :, None, None]), 0.0)
    total = jnp.sum(weights, axis=(3, 4))
    weights = weights.reshape(heads, qrows, krows)
    summed = jnp.einsum("hqk,khd->qhd", weights, values.astype(jnp.float32), precision=HIGH)
    return (top.reshape(heads, qrows), total.reshape(heads, qrows), summed)


def merge_parts(first, second):
    top_a, total_a, summed_a = first
    top_b, total_b, summed_b = second
    best = jnp.maximum(top_a, top_b)
    keep_a = jnp.exp(top_a - best)
    keep_b = jnp.exp(top_b - best)
    merged = summed_a * keep_a.T[:, :, None] + summed_b * keep_b.T[:, :, None]
    return (best, total_a * keep_a + total_b * keep_b, merged)


def on_device(
    x_first, x_second, stale_kv, w_qkv, w_out, q_gain, k_gain, layout, counts, slot_block
):
    me = lax.axis_index("pipe")
    tokens = BPM * BLOCK
    heads = w_qkv.shape[2] // HS
    width = heads * HS
    scale = 1.0 / math.sqrt(HS)
    linked = slot_mask(layout, counts, slot_block)
    total_blocks = linked.shape[0]
    block_ids = jnp.arange(total_blocks, dtype=jnp.int32)
    batch_of = block_ids // BPM
    mine = lax.dynamic_slice_in_dim(linked, me * BPM, BPM, 0)
    own = lax.dynamic_slice_in_dim(mine, me * BPM, BPM, 1)
    remote = mine & (batch_of != me)[None, :]

    def step(x_rows, prior_k, prior_v):
        raw = jnp.einsum(
            "rd,cdh->crh",
            lax.all_gather(x_rows, "seq", axis=0, tiled=True),
            w_qkv,
            preferred_element_type=jnp.float32,
        )
        query = normalize(raw[0], q_gain, HS).astype(jnp.bfloat16)
        keys = normalize(raw[1], k_gain, HS).astype(jnp.bfloat16)
        values = raw[2].astype(jnp.bfloat16)
        query_h = query.reshape(tokens, heads, HS)
        start_part = partial_attend(
            query_h, keys.reshape(tokens, heads, HS), values.reshape(tokens, heads, HS), own, scale
        )
        piece_k = lax.all_gather(prior_k, "pipe", axis=0, tiled=True)
        piece_v = lax.all_gather(prior_v, "pipe", axis=0, tiled=True)
        count = piece_k.shape[0]
        fresh = partial_attend(
            query_h,
            piece_k.reshape(count, heads, HS),
            piece_v.reshape(count, heads, HS),
            remote,
            scale,
        )
        best, denom_h, numer = merge_parts(start_part, fresh)
        denom = denom_h.T
        attn = (numer / denom[:, :, None]).reshape(tokens, width).astype(jnp.bfloat16)
        out = lax.psum_scatter(
            jnp.dot(attn, w_out, preferred_element_type=jnp.float32).astype(jnp.bfloat16),
            "seq",
            scatter_dimension=0,
            tiled=True,
        )
        return (out, keys, values)

    out_first, keys_first, values_first = step(x_first, stale_kv[0], stale_kv[1])
    out_second, unused_k, unused_v = step(x_second, keys_first, values_first)
    return (out_first, out_second)


def solution(mesh):
    placed = (
        P(("pipe", "seq"), None),
        P(("pipe", "seq"), None),
        P(None, "pipe", "seq"),
        P(None, None, "seq"),
        P("seq", None),
        P("seq"),
        P("seq"),
        P(),
        P(),
        P(),
    )
    return jax.shard_map(
        on_device,
        mesh=mesh,
        in_specs=placed,
        out_specs=(P(("pipe", "seq"), None), P(("pipe", "seq"), None)),
        check_vma=False,
    )
```

profile of v0, /device:TPU:8, one launch (start us, length us, event | category | flops | bytes accessed | tf_op | source)
XLA Modules:
  0.0 786.6 jit_solution(18196252297809986685)
XLA Ops:
  7.2 0.0 all-gather.8.cloned.1.call-start
  7.3 37.1 %all_gather.18 = bf16[128,2560]{1,0:T(8,128)(2,1)S(1)} all-gather(bf16[8,2560]{1,0:T(8,128)(2,1)} %param.10), channel_id=1, replica_groups=mesh['pipe'=32,'seq'=16] {'seq'}, dimensions={0}, use_global_device_ids=true | all-gather | bytes 696320 | tf_op jit(solution)/shard_map/all_gather | solution.py:80
  44.4 0.7 convolution_bitcast_fusion.1
  45.2 1.3 fusion.32
  46.5 0.0 all-gather.8.cloned.1.call-update
  46.5 0.0 all-gather.10.cloned.1.call-start
  46.6 1.4 fusion.62
  48.0 0.0 all-gather.10.cloned.1.call-update
  48.0 0.0 all-gather.14.cloned.1.call-start
  48.1 0.6 slice.43
  48.7 0.1 all-gather.14.cloned.1.call-update
  48.8 0.0 all-gather.12.cloned.1.call-start
  48.8 0.5 all-gather.12.cloned.1.call-update
  49.3 0.0 reduce-scatter.5.cloned.1.call-start
  49.4 0.1 mul.181
  49.5 27.8 %all_gather.21 = bf16[128,2560]{1,0:T(8,128)(2,1)S(1)} all-gather(bf16[8,2560]{1,0:T(8,128)(2,1)S(1)} %copy-done.5), channel_id=1, replica_groups=mesh['pipe'=32,'seq'=16] {'seq'}, dimensions={0}, use_global_device_ids=true | all-gather | bytes 696320 | tf_op jit(solution)/shard_map/all_gather | solution.py:80
  77.3 0.7 convolution_bitcast_fusion
  78.1 0.1 copy.20
  78.1 0.1 iota_compare_fusion.1
  78.2 0.2 convert_reduce_fusion
  78.5 0.2 fusion.43
  78.6 0.2 convolution_compare_fusion
  78.9 0.7 dynamic_slice.6
  79.6 0.1 mul.175
  79.8 0.1 broadcast_bitcast_fusion
  79.8 1.0 fusion.65
  80.8 1.0 fusion.66
  81.8 0.7 fusion.29
  82.5 85.6 %all-gather.8.cloned.1.call-done = bf16[4096,128]{0,1:T(8,128)(2,1)} async-done(((bf16[128,128]{0,1:T(8,128)(2,1)}), bf16[4096,128]{0,1:T(8,128)(2,1)}) %all-gather.8.cloned.1.call-update) | async-done | bytes 1048592 | tf_op jit(solution)/shard_map/all_gather | solution.py:91
  168.1 4.0 fusion.64
  172.1 144.8 %all-gather.10.cloned.1.call-done = bf16[1,4096,128]{2,1,0:T(8,128)(2,1)} async-done(((bf16[1,128,128]{2,1,0:T(8,128)(2,1)}), bf16[1,4096,128]{2,1,0:T(8,128)(2,1)}) %all-gather.10.cloned.1.call-update) | async-done | bytes 1048592 | tf_op jit(solution)/shard_map/all_gather | solution.py:91
  317.0 1.5 copy.22
  318.5 0.9 fusion.63
  319.4 1.9 copy-done.1
  321.4 1.6 fusion.4
  323.0 124.8 %all-gather.14.cloned.1.call-done = bf16[1,4096,128]{1,2,0:T(8,128)(2,1)} async-done(((bf16[1,128,128]{1,2,0:T(8,128)(2,1)}), bf16[1,4096,128]{1,2,0:T(8,128)(2,1)}) %all-gather.14.cloned.1.call-update) | async-done | bytes 1048592 | tf_op jit(solution)/shard_map/all_gather | solution.py:92
  447.9 5.6 fusion.23
  453.5 0.9 fusion.24
  454.4 1.2 convolution_convert_fusion
  455.6 0.0 reduce-scatter.5.cloned.1.call-update
  455.6 0.2 reduce-scatter.3.cloned.1.call-start
  455.8 140.8 %all-gather.12.cloned.1.call-done = bf16[1,4096,128]{2,1,0:T(8,128)(2,1)} async-done(((bf16[1,128,128]{2,1,0:T(8,128)(2,1)}), bf16[1,4096,128]{2,1,0:T(8,128)(2,1)}) %all-gather.12.cloned.1.call-update) | async-done | bytes 1048592 | tf_op jit(solution)/shard_map/all_gather | solution.py:92
  596.7 2.3 copy.23
  599.0 5.5 fusion.22
  604.5 0.9 fusion.25
  605.4 1.2 convolution_convert_fusion.1
  606.6 85.7 %reduce-scatter.5.cloned.1.call-done = bf16[8,2560]{1,0:T(8,128)(2,1)} async-done(((bf16[128,2560]{1,0:T(8,128)(2,1)}), bf16[8,2560]{1,0:T(8,128)(2,1)}) %reduce-scatter.5.cloned.1.call-update) | async-done | bytes 40976 | tf_op jit(solution)/shard_map/reduce_scatter | solution.py:104
  692.3 87.4 %reduce-scatter.3.cloned.1.call-done = bf16[8,2560]{1,0:T(8,128)(2,1)} async-done(((bf16[128,2560]{1,0:T(8,128)(2,1)}), bf16[8,2560]{1,0:T(8,128)(2,1)}) %reduce-scatter.3.cloned.1.call-update) | async-done | bytes 40976 | tf_op jit(solution)/shard_map/reduce_scatter | solution.py:104
  (36 shorter events, 0.3 us)
Async XLA Ops:
  7.2 37.2 %copy-start = (bf16[3,2560,128]{2,1,0:T(8,128)(2,1)S(1)}, bf16[3,2560,128]{2,1,0:T(8,128)(2,1)}, u32[]{:S(2)}) copy-start(bf16[3,2560,128]{2,1,0:T(8,128)(2,1)} %param.13) | copy-start | bytes 5898244
  7.2 42.2 %copy-start.7 = (f32[128]{0:T(128)S(1)}, f32[128]{0:T(128)}, u32[]{:S(2)}) copy-start(f32[128]{0:T(128)} %param.16) | copy-start | bytes 1540
  7.2 42.3 %copy-start.5 = (bf16[8,2560]{1,0:T(8,128)(2,1)S(1)}, bf16[8,2560]{1,0:T(8,128)(2,1)}, u32[]{:S(2)}) copy-start(bf16[8,2560]{1,0:T(8,128)(2,1)} %param.11) | copy-start | bytes 122884
  7.2 70.9 %copy-start.6 = (s32[32,16]{0,1:T(8,128)S(1)}, s32[32,16]{0,1:T(8,128)}, u32[]{:S(2)}) copy-start(s32[32,16]{0,1:T(8,128)} %param.17) | copy-start | bytes 6148
  7.2 70.9 %copy-start.8 = (s32[32]{0:T(128)S(1)}, s32[32]{0:T(128)}, u32[]{:S(2)}) copy-start(s32[32]{0:T(128)} %param.18) | copy-start | bytes 388
  7.2 71.2 %copy-start.9 = (s32[32]{0:T(128)S(1)}, s32[32]{0:T(128)}, u32[]{:S(2)}) copy-start(s32[32]{0:T(128)} %param.19) | copy-start | bytes 388
  7.2 72.4 %copy-start.10 = (f32[128]{0:T(128)S(1)}, f32[128]{0:T(128)}, u32[]{:S(2)}) copy-start(f32[128]{0:T(128)} %param.15) | copy-start | bytes 1540
  7.2 160.8 %all-gather.8.cloned.1.call-start = ((), (), s32[]{:S(2)}) async-start(), calls=%async_computation.3 | async-start | bytes 1081344 | tf_op jit(solution)/shard_map/all_gather | solution.py:91
  46.5 270.4 %all-gather.10.cloned.1.call-start = ((), (), s32[]{:S(2)}) async-start(), calls=%async_computation.5 | async-start | bytes 1081344 | tf_op jit(solution)/shard_map/all_gather | solution.py:91
  48.0 399.9 %all-gather.14.cloned.1.call-start = ((), (), s32[]{:S(2)}) async-start(), calls=%async_computation.7 | async-start | bytes 1081344 | tf_op jit(solution)/shard_map/all_gather | solution.py:92
  48.8 547.9 %all-gather.12.cloned.1.call-start = ((), (), s32[]{:S(2)}) async-start(), calls=%async_computation.6 | async-start | bytes 1081344 | tf_op jit(solution)/shard_map/all_gather | solution.py:92
  49.3 642.9 %reduce-scatter.5.cloned.1.call-start = ((), (), s32[]{:S(2)}) async-start(), calls=%async_computation.4 | async-start | bytes 696320 | tf_op jit(solution)/shard_map/reduce_scatter | solution.py:104
  318.5 2.9 copy-start.1
  319.4 3.6 copy-start.2
  323.0 131.3 %copy-start.3 = (bf16[128,2560]{1,0:T(8,128)(2,1)S(1)}, bf16[128,2560]{1,0:T(8,128)(2,1)}, u32[]{:S(2)}) copy-start(bf16[128,2560]{1,0:T(8,128)(2,1)} %param.14) | copy-start | bytes 1966084
  455.6 148.9 %copy-start.4 = (bf16[1,128,128]{1,2,0:T(8,128)(2,1)S(1)}, bf16[1,128,128]{1,2,0:T(8,128)(2,1)}, u32[]{:S(2)}) copy-start(bf16[1,128,128]{1,2,0:T(8,128)(2,1)} %slice.43) | copy-start | bytes 98308
  455.6 324.1 %reduce-scatter.3.cloned.1.call-start = ((), (), s32[]{:S(2)}) async-start(), calls=%async_computation.2 | async-start | bytes 696320 | tf_op jit(solution)/shard_map/reduce_scatter | solution.py:104
Sparse Core Ops, SparseCore 0:
  46.7 121.3 all-gather.7
  170.7 146.1 all-gather.9
  319.0 128.8 all-gather.13
  450.4 146.2 all-gather.11
  601.7 90.4 reduce-scatter.4
  697.3 82.3 reduce-scatter.2
where the time goes:
time: 787 us
  waiting for transfers between devices  670 us (85%)
  blocking collectives  64.9 us (8%)
  matrix products  24 us (3%)
  between operations  14.4 us (2%)
  local copies, waits for them, and re-layouts  8.75 us (1%)
    all_gather x2, waiting for transfers between devices, step(): piece_v = lax.all_gather(prior_v, 'pipe', axis=0, tiled=True)  266 us
    all_gather x2, waiting for transfers between devices, step(): piece_k = lax.all_gather(prior_k, 'pipe', axis=0, tiled=True)  230 us
    reduce_scatter x2, waiting for transfers between devices, step(): lax.psum_scatter(jnp.dot(attn, w_out, preferred_element_type=jnp.float32)...  173 us
    all_gather x2, blocking collectives, step(): lax.all_gather(x_rows, 'seq', axis=0, tiled=True)  64.9 us
  transfers between devices with their start and end apart: 6, of which 6 were waited for; matrix products, arithmetic and copies ran while one was open for 4% of the time, Pallas kernels for 0%

commit v1 on v0

--- a/solution.py
+++ b/solution.py
@@ -88,7 +88,15 @@
         start_part = partial_attend(
             query_h, keys.reshape(tokens, heads, HS), values.reshape(tokens, heads, HS), own, scale
         )
-        piece_k = lax.all_gather(prior_k, "pipe", axis=0, tiled=True)
+        piece_k = jnp.concatenate(
+            lax.all_to_all(
+                jnp.stack([prior_k] * lax.axis_size("pipe"), axis=0),
+                axis_name="pipe",
+                split_axis=0,
+                concat_axis=0,
+            ),
+            axis=0,
+        )
         piece_v = lax.all_gather(prior_v, "pipe", axis=0, tiled=True)
         count = piece_k.shape[0]
         fresh = partial_attend(

time: 787 us -> 548 us (0.70)
  waiting for transfers between devices: 670 us -> 382 us
  blocking collectives: 64.9 us -> 86.7 us
  starting transfers between devices: 0.42 us -> 20.7 us
  local copies, waits for them, and re-layouts: 8.75 us -> 17.5 us
    all_gather x2 -> x0, waiting for transfers between devices: 230 us -> none  [step(): piece_k = lax.all_gather(prior_k, 'pipe', axis=0, tiled=True)]
    all_gather x2, waiting for transfers between devices: 266 us -> 190 us  [step(): piece_v = lax.all_gather(prior_v, 'pipe', axis=0, tiled=True)]
    all_gather x2, blocking collectives: 64.9 us -> 86.7 us  [step(): lax.all_gather(x_rows, 'seq', axis=0, tiled=True)]
    all_to_all x0 -> x2, starting transfers between devices: none -> 20.3 us  [step(): lax.all_to_all(jnp.stack([prior_k] * lax.axis_size('pipe'), axis=0), axis...]
    all_to_all x0 -> x2, waiting for transfers between devices: none -> 17.9 us  [step(): lax.all_to_all(jnp.stack([prior_k] * lax.axis_size('pipe'), axis=0), axis...]
  transfers between devices with their start and end apart: 6 -> 6, of which waited for: 6 -> 5; matrix products, arithmetic and copies ran while one was open for 4% -> 7% of each run, Pallas kernels for 0% -> 0%
where the time goes in v1:
time: 548 us; the launch traced here: 547 us
  waiting for transfers between devices  382 us (70%)
  blocking collectives  86.7 us (16%)
  matrix products  22.8 us (4%)
  starting transfers between devices  20.7 us (4%)
  local copies, waits for them, and re-layouts  17.5 us (3%)
  between operations  14.1 us (3%)
    all_gather x2, waiting for transfers between devices, step(): piece_v = lax.all_gather(prior_v, 'pipe', axis=0, tiled=True)  190 us
    reduce_scatter x2, waiting for transfers between devices, step(): lax.psum_scatter(jnp.dot(attn, w_out, preferred_element_type=jnp.float32)...  173 us
    all_gather x2, blocking collectives, step(): lax.all_gather(x_rows, 'seq', axis=0, tiled=True)  86.7 us
    all_to_all x2, starting transfers between devices, step(): lax.all_to_all(jnp.stack([prior_k] * lax.axis_size('pipe'), axis=0), axis...  20.3 us
    all_to_all x2, waiting for transfers between devices, step(): lax.all_to_all(jnp.stack([prior_k] * lax.axis_size('pipe'), axis=0), axis...  17.9 us
    dot_general x4, matrix products, partial_attend(): jnp.einsum('hqk,khd->qhd', weights, values.astype(jnp.float32), precision...  12.9 us
  transfers between devices with their start and end apart: 6, of which 5 were waited for; matrix products, arithmetic and copies ran while one was open for 7% of the time, Pallas kernels for 0%

profile of v1, /device:TPU:8, one launch (start us, length us, event | category | flops | bytes accessed | tf_op | source)
XLA Modules:
  0.0 547.1 jit_solution(12383812722902590313)
XLA Ops:
  7.3 37.1 %all_gather.12 = bf16[128,2560]{1,0:T(8,128)(2,1)S(1)} all-gather(bf16[8,2560]{1,0:T(8,128)(2,1)} %param.10), channel_id=1, replica_groups=mesh['pipe'=32,'seq'=16] {'seq'}, dimensions={0}, use_global_device_ids=true | all-gather | bytes 696320 | tf_op jit(solution)/shard_map/all_gather | solution.py:80
  44.4 0.7 convolution_bitcast_fusion.1
  45.1 0.6 slice.47
  45.7 1.4 slice_bitcast_fusion
  47.1 0.1 copy.31
  47.2 1.2 stack.6
  48.5 10.7 %all-to-all-start = ((bf16[32,128,128]{1,2,0:T(8,128)(2,1)}), bf16[32,128,128]{1,2,0:T(8,128)(2,1)S(1)}, u32[]{:S(2)}, u32[]{:S(2)}) async-start(bf16[32,128,128]{1,2,0:T(8,128)(2,1)} %stack.6), calls=%async_computation | async-start | bytes 2097152 | tf_op jit(solution)/shard_map/all_to_all | solution.py:92
  59.2 0.7 all-gather.5.cloned.1.call-update
  59.9 0.1 copy.29
  60.0 0.1 mul.183
  60.1 0.1 fusion.32
  60.2 0.1 mul.177
  60.3 49.6 %all_gather.14 = bf16[128,2560]{1,0:T(8,128)(2,1)S(1)} all-gather(bf16[8,2560]{1,0:T(8,128)(2,1)S(1)} %copy-done.5), channel_id=1, replica_groups=mesh['pipe'=32,'seq'=16] {'seq'}, dimensions={0}, use_global_device_ids=true | all-gather | bytes 696320 | tf_op jit(solution)/shard_map/all_gather | solution.py:80
  109.9 0.7 convolution_bitcast_fusion
  110.7 0.1 iota_compare_fusion.1
  110.7 0.2 convert_reduce_fusion
  111.0 0.2 fusion.43
  111.2 0.2 convolution_compare_fusion
  111.4 0.7 dynamic_slice.6
  112.2 1.3 stack.8
  113.4 9.7 %all-to-all-start.1 = ((bf16[32,128,128]{1,2,0:T(8,128)(2,1)}), bf16[32,128,128]{1,2,0:T(8,128)(2,1)}, u32[]{:S(2)}, u32[]{:S(2)}) async-start(bf16[32,128,128]{1,2,0:T(8,128)(2,1)} %stack.8), calls=%async_computation.2 | async-start | bytes 2097152 | tf_op jit(solution)/shard_map/all_to_all | solution.py:92
  123.1 0.2 reduce-scatter.5.cloned.1.call-start
  123.3 0.7 and_bitcast_fusion
  124.1 1.0 fusion.63
  125.1 1.0 fusion.64
  126.0 0.7 fusion.29
  126.8 0.1 broadcast_bitcast_fusion
  126.8 1.7 copy.32
  128.5 1.5 reshape_reshape.6
  130.1 2.8 fusion.61
  132.8 17.9 %all-to-all-done.1 = bf16[32,128,128]{1,2,0:T(8,128)(2,1)} async-done(((bf16[32,128,128]{1,2,0:T(8,128)(2,1)}), bf16[32,128,128]{1,2,0:T(8,128)(2,1)}, u32[]{:S(2)}, u32[]{:S(2)}) %all-to-all-start.1) | async-done | bytes 1048608 | tf_op jit(solution)/shard_map/all_to_all | solution.py:92
  150.7 2.9 copy.36
  153.6 1.5 reshape_reshape.7
  155.1 0.9 fusion.62
  156.1 1.9 copy-done.2
  158.0 1.6 fusion.4
  159.7 52.6 %all-gather.7.cloned.1.call-done = bf16[1,4096,128]{1,2,0:T(8,128)(2,1)} async-done(((bf16[1,128,128]{1,2,0:T(8,128)(2,1)}), bf16[1,4096,128]{1,2,0:T(8,128)(2,1)}) %all-gather.7.cloned.1.call-update) | async-done | bytes 1048592 | tf_op jit(solution)/shard_map/all_gather | solution.py:100
  212.3 5.6 %fusion.23 = f32[128,2,64]{0,2,1:T(8,128)S(1)} fusion(bf16[4096,2,64]{0,2,1:T(8,128)(2,1)} %bitcast.123, f32[2,128,4096]{2,1,0:T(8,128)} %copy-done.1, f32[2,128]{1,0:T(2,128)S(1)} %get-tuple-element.18, pred[4096]{0:T(1024)(128)(4,1)S(1)} %broadcast_bitcast_fusion, f32[128,2]{0,1:T(2,128)S(1)} %get-tuple-element.6), kind=kOutput, calls=%fused_computation.35 | convolution fusion | flops 807419904 | bytes 5314560 | tf_op jit(solution)/shard_map/hqk,khd->qhd/dot_general | solution.py:47
  217.9 0.9 fusion.24
  218.8 1.2 convolution_convert_fusion
  220.1 0.0 reduce-scatter.3.cloned.1.call-start
  220.1 137.3 %all-gather.5.cloned.1.call-done = bf16[1,4096,128]{2,1,0:T(8,128)(2,1)} async-done(((bf16[1,128,128]{2,1,0:T(8,128)(2,1)}), bf16[1,4096,128]{2,1,0:T(8,128)(2,1)}) %all-gather.5.cloned.1.call-update) | async-done | bytes 1048592 | tf_op jit(solution)/shard_map/all_gather | solution.py:100
  357.4 2.3 copy.33
  359.7 5.5 %fusion.22 = f32[128,2,64]{0,2,1:T(8,128)S(1)} fusion(bf16[4096,2,64]{0,2,1:T(8,128)(2,1)} %bitcast.122, f32[2,128,4096]{2,1,0:T(8,128)} %get-tuple-element.17, f32[2,128]{1,0:T(2,128)S(1)} %get-tuple-element.16, pred[4096]{0:T(1024)(128)(4,1)S(1)} %broadcast_bitcast_fusion, f32[128,2]{0,1:T(2,128)S(1)} %get-tuple-element.9), kind=kOutput, calls=%fused_computation.34 | convolution fusion | flops 807419904 | bytes 5314560 | tf_op jit(solution)/shard_map/hqk,khd->qhd/dot_general | solution.py:47
  365.2 0.9 fusion.25
  366.1 1.2 convolution_convert_fusion.1
  367.3 85.8 %reduce-scatter.5.cloned.1.call-done = bf16[8,2560]{1,0:T(8,128)(2,1)} async-done(((bf16[128,2560]{1,0:T(8,128)(2,1)}), bf16[8,2560]{1,0:T(8,128)(2,1)}) %reduce-scatter.5.cloned.1.call-update) | async-done | bytes 40976 | tf_op jit(solution)/shard_map/reduce_scatter | solution.py:112
  453.1 87.4 %reduce-scatter.3.cloned.1.call-done = bf16[8,2560]{1,0:T(8,128)(2,1)} async-done(((bf16[128,2560]{1,0:T(8,128)(2,1)}), bf16[8,2560]{1,0:T(8,128)(2,1)}) %reduce-scatter.3.cloned.1.call-update) | async-done | bytes 40976 | tf_op jit(solution)/shard_map/reduce_scatter | solution.py:112
  (42 shorter events, 0.4 us)
Async XLA Ops:
  7.2 37.2 %copy-start = (bf16[3,2560,128]{2,1,0:T(8,128)(2,1)S(1)}, bf16[3,2560,128]{2,1,0:T(8,128)(2,1)}, u32[]{:S(2)}) copy-start(bf16[3,2560,128]{2,1,0:T(8,128)(2,1)} %param.13) | copy-start | bytes 5898244
  7.2 52.7 %copy-start.6 = (s32[32,16]{0,1:T(8,128)S(1)}, s32[32,16]{0,1:T(8,128)}, u32[]{:S(2)}) copy-start(s32[32,16]{0,1:T(8,128)} %param.17) | copy-start | bytes 6148
  7.2 52.8 %copy-start.7 = (f32[128]{0:T(128)S(1)}, f32[128]{0:T(128)}, u32[]{:S(2)}) copy-start(f32[128]{0:T(128)} %param.16) | copy-start | bytes 1540
  7.2 53.0 %copy-start.10 = (f32[128]{0:T(128)S(1)}, f32[128]{0:T(128)}, u32[]{:S(2)}) copy-start(f32[128]{0:T(128)} %param.15) | copy-start | bytes 1540
  7.2 53.1 %copy-start.5 = (bf16[8,2560]{1,0:T(8,128)(2,1)S(1)}, bf16[8,2560]{1,0:T(8,128)(2,1)}, u32[]{:S(2)}) copy-start(bf16[8,2560]{1,0:T(8,128)(2,1)} %param.11) | copy-start | bytes 122884
  7.2 205.1 %all-gather.7.cloned.1.call-start = ((), (), s32[]{:S(2)}) async-start(), calls=%async_computation.7 | async-start | bytes 1081344 | tf_op jit(solution)/shard_map/all_gather | solution.py:100
  45.1 65.6 %copy-start.8 = (s32[32]{0:T(128)S(1)}, s32[32]{0:T(128)}, u32[]{:S(2)}) copy-start(s32[32]{0:T(128)} %param.18) | copy-start | bytes 388
  45.1 65.9 %copy-start.11 = (s32[32]{0:T(128)S(1)}, s32[32]{0:T(128)}, u32[]{:S(2)}) copy-start(s32[32]{0:T(128)} %param.19) | copy-start | bytes 388
  48.5 63.7 %all-to-all-start = ((bf16[32,128,128]{1,2,0:T(8,128)(2,1)}), bf16[32,128,128]{1,2,0:T(8,128)(2,1)S(1)}, u32[]{:S(2)}, u32[]{:S(2)}) async-start(bf16[32,128,128]{1,2,0:T(8,128)(2,1)} %stack.6), calls=%async_computation | async-start | bytes 2097152 | tf_op jit(solution)/shard_map/all_to_all | solution.py:92
  59.1 298.3 %all-gather.5.cloned.1.call-start = ((), (), s32[]{:S(2)}) async-start(), calls=%async_computation.6 | async-start | bytes 1081344 | tf_op jit(solution)/shard_map/all_gather | solution.py:100
  111.4 0.7 copy-start.9
  113.4 37.3 %all-to-all-start.1 = ((bf16[32,128,128]{1,2,0:T(8,128)(2,1)}), bf16[32,128,128]{1,2,0:T(8,128)(2,1)}, u32[]{:S(2)}, u32[]{:S(2)}) async-start(bf16[32,128,128]{1,2,0:T(8,128)(2,1)} %stack.8), calls=%async_computation.2 | async-start | bytes 2097152 | tf_op jit(solution)/shard_map/all_to_all | solution.py:92
  123.1 330.0 %reduce-scatter.5.cloned.1.call-start = ((), (), s32[]{:S(2)}) async-start(), calls=%async_computation.5 | async-start | bytes 696320 | tf_op jit(solution)/shard_map/reduce_scatter | solution.py:112
  155.1 2.9 copy-start.2
  156.1 3.6 copy-start.1
  159.7 59.1 %copy-start.3 = (bf16[128,2560]{1,0:T(8,128)(2,1)S(1)}, bf16[128,2560]{1,0:T(8,128)(2,1)}, u32[]{:S(2)}) copy-start(bf16[128,2560]{1,0:T(8,128)(2,1)} %param.14) | copy-start | bytes 1966084
  220.0 145.2 %copy-start.4 = (bf16[1,128,128]{1,2,0:T(8,128)(2,1)S(1)}, bf16[1,128,128]{1,2,0:T(8,128)(2,1)}, u32[]{:S(2)}) copy-start(bf16[1,128,128]{1,2,0:T(8,128)(2,1)} %slice.47) | copy-start | bytes 98308
  220.1 320.5 %reduce-scatter.3.cloned.1.call-start = ((), (), s32[]{:S(2)}) async-start(), calls=%async_computation.4 | async-start | bytes 696320 | tf_op jit(solution)/shard_map/reduce_scatter | solution.py:112
Sparse Core Ops, SparseCore 0:
  45.9 166.4 all-gather.6
  215.0 142.4 all-gather.4
  362.6 90.4 reduce-scatter.4
  458.2 82.3 reduce-scatter.2
